TPU v7x, 32 devices: a whole 2x2x4 slice. The times are simulated.
32 devices in a mesh: row: 8 (over z, y), col: 4 (over x, core).
Axes of the slice: x: 2, y: 2, z: 4, core: 2. Of those that a mesh axis runs over, the one named last changes fastest.
Arguments:
- tokens: bfloat16 [1024, 4096], P('row'), may hold values from -6 to 6
- in_weight: bfloat16 [4096, 8192], P('row', 'col'), may hold values from -0.09375 to 0.09375
- gate_branch: bfloat16 [1024, 8192], P('row', 'col'), may hold values from -6 to 6
- conv_weight: float32 [4, 8192], P(None, 'col'), may hold values from -3 to 3
- out_weight: bfloat16 [8192, 4096], P('col'), may hold values from -0.0625 to 0.0625
- target: bfloat16 [1024, 4096], P('row'), may hold values from -6 to 6
- lang_ids: int32 [1024], P('row'), may hold values from 0 to 31
- lang_weight: float32 [32], replicated, may hold values from 0.25 to 4
- doc_pos: int32 [1024], P('row'), may hold values from 0 to 127, as said below
Outputs:
- block_out: bfloat16 [1024, 4096], P('row', 'col')
- grad_tokens: bfloat16 [1024, 4096], P('row', 'col')
- grad_gate: bfloat16 [1024, 8192], P('row', 'col')
Inputs may be any that keep to these rules, and one draw needn't show every extreme that they name: doc_pos is 0 at the first token and at every document's first token, and otherwise one more than the previous token's; no document is longer than 128 tokens and one is exactly 128 tokens long; apart from token 0, no document begins within the first 4 tokens of an aligned block of 128 tokens.
All inputs are finite; a program needn't handle non-finite values.
Results may differ from a plain program's by a relative error of at most 0.022.
Values may be sent and summed in bfloat16 or wider, within the bound.
No kernel may reach another device: no remote copies, remote signals or barrier semaphores. Data moves between devices by JAX's collectives and lax.ppermute only.
A program may use at most 128 MiB of HBM per device.

v0:
```python
import jax
import jax.numpy as jnp
from jax import lax
from jax.sharding import PartitionSpec as P

CONV = 4
LANGS = 32


def passed_along(value, axis, steps):
    count = lax.axis_size(axis)
    first, last = (max(0, -steps), min(count, count - steps))
    return lax.ppermute(value, axis, [(source, source + steps) for source in range(first, last)])


def silu_grad(argument):
    sigmoid_v = jax.nn.sigmoid(argument)
    return sigmoid_v * (1.0 + argument * (1.0 - sigmoid_v))


def shards(
    tokens, in_weight, gate_branch, conv_weight, out_weight, target, lang_ids, lang_weight, doc_pos
):
    row_count = tokens.shape[0]
    inner_width = gate_branch.shape[1]
    margin = CONV - 1
    full_in = lax.all_gather(in_weight, "row", axis=0, tiled=True)
    inner_x = jnp.dot(tokens, full_in, preferred_element_type=jnp.float32).astype(jnp.bfloat16)
    from_prev = passed_along(inner_x[row_count - margin :], "row", 1)
    extended = jnp.concatenate([from_prev, inner_x], axis=0).astype(jnp.float32)
    conv_sum = jnp.zeros((row_count, inner_width), jnp.float32)
    for offset in range(CONV):
        keep_mask = (doc_pos >= offset).astype(jnp.float32)[:, None]
        conv_sum = (
            conv_sum
            + conv_weight[offset][None, :]
            * extended[margin - offset : margin - offset + row_count]
            * keep_mask
        )
    gate_value = gate_branch.astype(jnp.float32)
    gate_act = jax.nn.silu(gate_value)
    conv_act = jax.nn.silu(conv_sum)
    mixed = (conv_act * gate_act).astype(jnp.bfloat16)
    partial_value = jnp.dot(mixed, out_weight, preferred_element_type=jnp.float32)
    columns = tokens.shape[1] // lax.axis_size("col")
    col_start = lax.axis_index("col") * columns
    lang_table = (lang_ids[:, None] == jnp.arange(LANGS, dtype=jnp.int32)[None, :]).astype(
        jnp.float32
    )
    token_weight = jnp.sum(lang_table * lang_weight[None, :], axis=1)[:, None]
    out_total = lax.psum(partial_value.astype(jnp.bfloat16), "col").astype(jnp.float32)
    out_block = lax.dynamic_slice_in_dim(out_total, col_start, columns, 1)
    residual_grad = (token_weight * (out_total - target.astype(jnp.float32))).astype(jnp.bfloat16)
    grad_mixed = lax.dot_general(
        residual_grad, out_weight, (((1,), (1,)), ((), ())), preferred_element_type=jnp.float32
    )
    grad_conv = grad_mixed * gate_act * silu_grad(conv_sum)
    grad_gate = (grad_mixed * conv_act * silu_grad(gate_value)).astype(jnp.bfloat16)
    local_grad = conv_weight[0][None, :] * grad_conv
    spill_over = jnp.zeros((margin, inner_width), jnp.float32)
    for offset in range(1, CONV):
        masked = (
            conv_weight[offset][None, :]
            * grad_conv
            * (doc_pos >= offset).astype(jnp.float32)[:, None]
        )
        local_grad = local_grad + jnp.concatenate(
            [masked[offset:], jnp.zeros((offset, inner_width), jnp.float32)], axis=0
        )
        spill_over = spill_over + jnp.concatenate(
            [jnp.zeros((margin - offset, inner_width), jnp.float32), masked[:offset]], axis=0
        )
    from_next = passed_along(spill_over, "row", -1)
    grad_x = (
        local_grad
        + jnp.concatenate(
            [jnp.zeros((row_count - margin, inner_width), jnp.float32), from_next], axis=0
        )
    ).astype(jnp.bfloat16)
    partial_grad = lax.dot_general(
        grad_x, full_in, (((1,), (1,)), ((), ())), preferred_element_type=jnp.float32
    )
    grad_tokens = lax.psum_scatter(
        partial_grad.astype(jnp.bfloat16), "col", scatter_dimension=1, tiled=True
    )
    return (out_block.astype(jnp.bfloat16), grad_tokens, grad_gate)


def solution(mesh):
    in_specs = (
        P("row", None),
        P("row", "col"),
        P("row", "col"),
        P(None, "col"),
        P("col", None),
        P("row", None),
        P("row"),
        P(),
        P("row"),
    )
    out_specs = (P("row", "col"), P("row", "col"), P("row", "col"))
    return jax.shard_map(shards, mesh=mesh, in_specs=in_specs, out_specs=out_specs, check_vma=False)
```

profile of v0, /device:TPU:0, one launch (start us, length us, event | category | flops | bytes accessed | tf_op | source)
XLA Modules:
  0.0 361.6 jit_solution(7084845556274055566)
XLA Ops:
  7.2 0.0 copy-start
  7.2 0.0 copy-start.3
  7.2 0.0 copy-start.5
  7.2 0.0 all-gather.2.cloned.1.call-start
  7.2 0.7 all-gather.2.cloned.1.call-update
  7.9 0.0 all-reduce.8.cloned.1.call-start
  8.0 0.9 fusion.22
  8.9 231.6 %all-gather.2.cloned.1.call-done = bf16[4096,2048]{1,0:T(8,128)(2,1)} async-done(((bf16[512,2048]{1,0:T(8,128)(2,1)}), bf16[4096,2048]{1,0:T(8,128)(2,1)}) %all-gather.2.cloned.1.call-update) | async-done | bytes 16777232 | tf_op jit(solution)/shard_map/all_gather | solution.py:27
  240.5 0.0 copy-done
  240.5 8.3 %convolution_convert_fusion.2 = bf16[128,2048]{1,0:T(8,128)(2,1)S(1)} fusion(bf16[128,4096]{1,0:T(8,128)(2,1)S(1)} %copy-done, bf16[4096,2048]{1,0:T(8,128)(2,1)} %all-gather.2.cloned.1.call-done), kind=kOutput, calls=%fused_computation.2 | convolution fusion | flops 2147745792 | bytes 18350080 | tf_op jit(solution)/shard_map/dot_general | solution.py:28
  248.8 2.7 collective-permute-start
  251.5 1.4 collective-permute-done
  252.9 0.1 maximum_convert_fusion
  253.1 0.7 fusion.9
  253.8 1.0 copy-done.2
  254.8 3.8 %convolution_convert_fusion.1 = bf16[128,4096]{1,0:T(8,128)(2,1)} fusion(bf16[2048,4096]{1,0:T(8,128)(2,1)S(1)} %copy-done.4, bf16[128,2048]{1,0:T(8,128)(2,1)S(1)} %copy-done.5, f32[128,2048]{1,0:T(8,128)S(1)} %fusion.9), kind=kOutput, calls=%fused_computation.1 | convolution fusion | flops 2150891520 | bytes 19398656 | tf_op jit(solution)/shard_map/dot_general | solution.py:44
  258.6 0.0 all-reduce.8.cloned.1.call-update
  258.6 0.0 reduce-scatter.2.cloned.1.call-start
  258.7 0.1 select_reduce_fusion
  258.8 36.9 %all-reduce.8.cloned.1.call-done = bf16[128,4096]{1,0:T(8,128)(2,1)} async-done(((bf16[128,4096]{1,0:T(8,128)(2,1)}), bf16[128,4096]{1,0:T(8,128)(2,1)}) %all-reduce.8.cloned.1.call-update) | async-done | bytes 1048592 | tf_op jit(solution)/shard_map/psum | solution.py:51
  295.7 13.7 %multiply_multiply_fusion.2 = (f32[128,2048]{1,0:T(8,128)S(1)}, f32[128,2048]{1,0:T(8,128)S(1)}, bf16[128,2048]{1,0:T(8,128)(2,1)}) fusion(f32[128]{0:T(128)S(1)} %get-tuple-element.13, f32[2048]{0:T(1024)S(1)} %bitcast.16, f32[128,2048]{1,0:T(8,128)} %copy-done.2, bf16[128,2048]{1,0:T(8,128)(2,1)} %param.11, bf16[2048,4096]{1,0:T(8,128)(2,1)} %param.13, ...), kind=kOutput, calls=%fused_computation.29 | convolution fusion | flops 2156396544 | bytes 23077888 | tf_op jit(solution)/shard_map/dot_general | solution.py:54
  309.4 0.3 multiply_multiply_fusion.1
  309.8 0.7 copy-done.1
  310.4 1.5 collective-permute-start.1
  311.9 1.3 slice.69
  313.2 1.1 slice.70
  314.3 1.1 slice.71
  315.4 0.8 collective-permute-done.1
  316.2 13.1 %convolution_convert_fusion = bf16[128,4096]{1,0:T(8,128)(2,1)} fusion(bf16[4096,2048]{1,0:T(8,128)(2,1)} %all-gather.2.cloned.1.call-done, f32[3,2048]{1,0:T(4,128)S(1)} %collective-permute-done.1, f32[125,2048]{1,0:T(8,128)} %slice.71, f32[126,2048]{1,0:T(8,128)} %slice.70, f32[127,2048]{1,0:T(8,128)S(1)} %slice.69, f32[128,2048]{1,0:T(8,128)S(1)} %get-tuple-element.4, ...), kind=kOutput, calls=%fused_computation | convolution fusion | flops 2149580800 | bytes 22003712 | tf_op jit(solution)/shard_map/dot_general | solution.py:80
  329.3 0.0 reduce-scatter.2.cloned.1.call-update
  329.3 1.7 dynamic-slice_convert_fusion
  331.0 24.1 %reduce-scatter.2.cloned.1.call-done = bf16[128,1024]{1,0:T(8,128)(2,1)} async-done(((bf16[128,4096]{1,0:T(8,128)(2,1)}), bf16[128,1024]{1,0:T(8,128)(2,1)}) %reduce-scatter.2.cloned.1.call-update) | async-done | bytes 262160 | tf_op jit(solution)/shard_map/reduce_scatter | solution.py:83
  (15 shorter events, 0.1 us)
Async XLA Ops:
  7.2 233.3 %copy-start = (bf16[128,4096]{1,0:T(8,128)(2,1)S(1)}, bf16[128,4096]{1,0:T(8,128)(2,1)}, u32[]{:S(2)}) copy-start(bf16[128,4096]{1,0:T(8,128)(2,1)} %param.9) | copy-start | bytes 3145732
  7.2 244.3 %copy-start.3 = (s32[128]{0:T(128)S(1)}, s32[128]{0:T(128)}, u32[]{:S(2)}) copy-start(s32[128]{0:T(128)} %param.17) | copy-start | bytes 1540
  7.2 247.6 %copy-start.5 = (bf16[128,2048]{1,0:T(8,128)(2,1)S(1)}, bf16[128,2048]{1,0:T(8,128)(2,1)}, u32[]{:S(2)}) copy-start(bf16[128,2048]{1,0:T(8,128)(2,1)} %param.11) | copy-start | bytes 1572868
  7.2 233.3 %all-gather.2.cloned.1.call-start = ((), (), s32[]{:S(2)}) async-start(), calls=%async_computation.1 | async-start | bytes 18874368 | tf_op jit(solution)/shard_map/all_gather | solution.py:27
  7.9 287.8 %all-reduce.8.cloned.1.call-start = ((), (), s32[]{:S(2)}) async-start(), calls=%async_computation.2 | async-start | bytes 2097152 | tf_op jit(solution)/shard_map/psum | solution.py:51
  240.5 14.3 %copy-start.4 = (bf16[2048,4096]{1,0:T(8,128)(2,1)S(1)}, bf16[2048,4096]{1,0:T(8,128)(2,1)}, u32[]{:S(2)}) copy-start(bf16[2048,4096]{1,0:T(8,128)(2,1)} %param.13) | copy-start | bytes 50331652
  248.8 4.2 %collective-permute-start = (bf16[3,2048]{1,0:T(4,128)(2,1)S(1)}, bf16[3,2048]{1,0:T(4,128)(2,1)S(1)}, u32[]{:S(2)}, u32[]{:S(2)}) collective-permute-start(bf16[3,2048]{1,0:T(4,128)(2,1)S(1)} %slice.64), channel_id=1, source_target_pairs={{0,4},{4,8},{8,12},{12,16},{16,20},{20,24},{24,28},{1,5},{5,9},{9,... | collective-permute-start | bytes 36872 | tf_op jit(solution)/shard_map/ppermute | solution.py:13
  253.8 1.0 copy-start.2
  254.8 3.8 %copy-start.6 = (f32[32]{0:T(128)S(1)}, f32[32]{0:T(128)}, u32[]{:S(2)}) copy-start(f32[32]{0:T(128)} %param.16) | copy-start | bytes 388
  254.8 3.9 %copy-start.7 = (s32[128]{0:T(128)S(1)}, s32[128]{0:T(128)}, u32[]{:S(2)}) copy-start(s32[128]{0:T(128)} %param.15) | copy-start | bytes 1540
  258.6 96.5 %reduce-scatter.2.cloned.1.call-start = ((), (), s32[]{:S(2)}) async-start(), calls=%async_computation.3 | async-start | bytes 1310720 | tf_op jit(solution)/shard_map/reduce_scatter | solution.py:83
  309.4 1.0 copy-start.1
  310.4 5.8 %collective-permute-start.1 = (f32[3,2048]{1,0:T(4,128)S(1)}, f32[3,2048]{1,0:T(4,128)S(1)}, u32[]{:S(2)}, u32[]{:S(2)}) collective-permute-start(f32[3,2048]{1,0:T(4,128)S(1)} %slice_add_fusion), channel_id=1, source_target_pairs={{4,0},{8,4},{12,8},{16,12},{20,16},{24,20},{28,24},{5,1},{9,5},{13... | collective-permute-start | bytes 73736 | tf_op jit(solution)/shard_map/ppermute | solution.py:13
Sparse Core Ops, SparseCore 0:
  10.2 230.2 all-gather.1
  258.8 36.9 all-reduce.7
  329.4 25.6 reduce-scatter.1
where the time goes:
time: 362 us
  waiting for transfers between devices  296 us (82%)
  matrix products  38.8 us (11%)
  between operations  13.9 us (4%)
  local copies, waits for them, and re-layouts  7.83 us (2%)
  starting transfers between devices  4.3 us (1%)
    all_gather x1, waiting for transfers between devices, shards(): full_in = lax.all_gather(in_weight, 'row', axis=0, tiled=True)  232 us
    psum x1, waiting for transfers between devices, shards(): lax.psum(partial_value.astype(jnp.bfloat16), 'col').astype(jnp.float32)  36.9 us
    reduce_scatter x1, waiting for transfers between devices, shards(): lax.psum_scatter(partial_grad.astype(jnp.bfloat16), 'col', scatter_dimens...  24.1 us
    dot_general x1, matrix products, shards(): lax.dot_general(residual_grad, out_weight, (((1,), (1,)), ((), ())), pref...  13.7 us
    dot_general x1, matrix products, shards(): lax.dot_general(grad_x, full_in, (((1,), (1,)), ((), ())), preferred_elem...  13.1 us
    dot_general x1, matrix products, shards(): jnp.dot(tokens, full_in, preferred_element_type=jnp.float32)  8.25 us
  transfers between devices with their start and end apart: 5, of which 5 were waited for; matrix products, arithmetic and copies ran while one was open for 2% of the time, Pallas kernels for 0%

commit v1 on v0

--- a/solution.py
+++ b/solution.py
@@ -1,3 +1,4 @@
+import functools
 import jax
 import jax.numpy as jnp
 from jax import lax
@@ -5,6 +6,41 @@
 
 CONV = 4
 LANGS = 32
+
+
+def pass_the_spans(packet, dimension_no):
+    packet = jnp.moveaxis(packet, 0, dimension_no)
+    b_now = packet.shape
+    return packet.reshape(
+        *b_now[:dimension_no],
+        b_now[dimension_no] * b_now[dimension_no + 1],
+        *b_now[dimension_no + 2 :]
+    )
+
+
+def spread_frame(array_here, along_axis, pos_dim):
+    q_n = lax.axis_size(along_axis)
+    nodes = [(ix, (ix + 1) % q_n) for ix in range(q_n)]
+    all_rows = [(dd, i0) for i0, dd in nodes]
+    part_now, r2 = ([], [])
+    for p in range(q_n - 1):
+        if p % 2 == 0:
+            part_now.append(
+                lax.ppermute(
+                    part_now[-1] if part_now else array_here, perm=nodes, axis_name=along_axis
+                )
+            )
+        else:
+            r2.append(
+                lax.ppermute(r2[-1] if r2 else array_here, axis_name=along_axis, perm=all_rows)
+            )
+    extra = jnp.stack([*part_now[::-1], array_here, *r2])
+    raw_out = lax.axis_index(along_axis) - len(part_now)
+    extra = extra[(jnp.arange(q_n) - raw_out) % q_n]
+    return pass_the_spans(extra, pos_dim)
+
+
+sector_choose = functools.partial(spread_frame, along_axis="row", pos_dim=0)
 
 
 def passed_along(value, axis, steps):
@@ -24,7 +60,7 @@
     row_count = tokens.shape[0]
     inner_width = gate_branch.shape[1]
     margin = CONV - 1
-    full_in = lax.all_gather(in_weight, "row", axis=0, tiled=True)
+    full_in = sector_choose(in_weight)
     inner_x = jnp.dot(tokens, full_in, preferred_element_type=jnp.float32).astype(jnp.bfloat16)
     from_prev = passed_along(inner_x[row_count - margin :], "row", 1)
     extended = jnp.concatenate([from_prev, inner_x], axis=0).astype(jnp.float32)

time: 362 us -> 503 us (1.39)
  waiting for transfers between devices: 296 us -> 367 us
  local copies, waits for them, and re-layouts: 7.83 us -> 50 us
  starting transfers between devices: 4.3 us -> 23.2 us
  other arithmetic: 1.27 us -> 9.09 us
    ppermute x0 -> x7, waiting for transfers between devices: none -> 306 us  [the longest x4 306 us: spread_frame(): lax.ppermute(part_now[-1] if part_now else array_here, perm=nodes, axis_n...]
    all_gather x1 -> x0, waiting for transfers between devices: 232 us -> none  [shards(): full_in = lax.all_gather(in_weight, 'row', axis=0, tiled=True)]
    gather x0 -> x3, local copies, waits for them, and re-layouts: none -> 22.6 us  [spread_frame(): extra = extra[(jnp.arange(q_n) - raw_out) % q_n]]
    unnamed x16 -> x29, local copies, waits for them, and re-layouts: 1.69 us -> 21.2 us
    ppermute x0 -> x7, starting transfers between devices: none -> 17.2 us  [the longest x3 9.15 us: spread_frame(): lax.ppermute(r2[-1] if r2 else array_here, axis_name=along_axis, perm=all...]
    unnamed x0 -> x1, other arithmetic: none -> 7.8 us
    dot_general x1, matrix products: 8.25 us -> 2.52 us  [shards(): jnp.dot(tokens, full_in, preferred_element_type=jnp.float32)]
    dot_general x1, matrix products: 3.76 us -> 9.46 us  [shards(): jnp.dot(mixed, out_weight, preferred_element_type=jnp.float32)]
  transfers between devices with their start and end apart: 5 -> 11, of which waited for: 5 -> 8; matrix products, arithmetic and copies ran while one was open for 2% -> 3% of each run, Pallas kernels for 0% -> 0%
where the time goes in v1:
time: 503 us; the launch traced here: 502 us
  waiting for transfers between devices  367 us (73%)
  local copies, waits for them, and re-layouts  50 us (10%)
  matrix products  38.7 us (8%)
  starting transfers between devices  23.2 us (5%)
  between operations  14.3 us (3%)
  other arithmetic  9.09 us (2%)
    ppermute x4, waiting for transfers between devices, spread_frame(): lax.ppermute(part_now[-1] if part_now else array_here, perm=nodes, axis_n...  306 us
    psum x1, waiting for transfers between devices, shards(): lax.psum(partial_value.astype(jnp.bfloat16), 'col').astype(jnp.float32)  34.6 us
    reduce_scatter x1, waiting for transfers between devices, shards(): lax.psum_scatter(partial_grad.astype(jnp.bfloat16), 'col', scatter_dimens...  23.9 us
    gather x3, local copies, waits for them, and re-layouts, spread_frame(): extra = extra[(jnp.arange(q_n) - raw_out) % q_n]  22.6 us
    unnamed x29, local copies, waits for them, and re-layouts  21.2 us
    dot_general x1, matrix products, shards(): lax.dot_general(residual_grad, out_weight, (((1,), (1,)), ((), ())), pref...  13.7 us
    dot_general x1, matrix products, shards(): lax.dot_general(grad_x, full_in, (((1,), (1,)), ((), ())), preferred_elem...  13.1 us
  transfers between devices with their start and end apart: 11, of which 8 were waited for; matrix products, arithmetic and copies ran while one was open for 3% of the time, Pallas kernels for 0%

profile of v1, /device:TPU:0, one launch (start us, length us, event | category | flops | bytes accessed | tf_op | source)
XLA Modules:
  0.0 502.4 jit_solution(760550495808361924)
XLA Ops:
  7.2 3.0 collective-permute-start
  10.3 48.9 %collective-permute-done = bf16[512,2048]{1,0:T(8,128)(2,1)S(1)} collective-permute-done((bf16[512,2048]{1,0:T(8,128)(2,1)}, bf16[512,2048]{1,0:T(8,128)(2,1)S(1)}, u32[]{:S(2)}, u32[]{:S(2)}) %collective-permute-start) | collective-permute-done | bytes 2097184 | tf_op jit(solution)/shard_map/ppermute | solution.py:29
  60.5 4.7 collective-permute-start.4
  65.2 84.8 %collective-permute-done.1 = bf16[512,2048]{1,0:T(8,128)(2,1)S(1)} collective-permute-done((bf16[512,2048]{1,0:T(8,128)(2,1)S(1)}, bf16[512,2048]{1,0:T(8,128)(2,1)S(1)}, u32[]{:S(2)}, u32[]{:S(2)}) %collective-permute-start.1) | collective-permute-done | bytes 2097184 | tf_op jit(solution)/shard_map/ppermute | solution.py:29
  150.0 1.4 copy-done.4
  151.4 2.5 collective-permute-start.2
  153.9 2.2 collective-permute-start.5
  156.1 86.4 %collective-permute-done.2 = bf16[512,2048]{1,0:T(8,128)(2,1)} collective-permute-done((bf16[512,2048]{1,0:T(8,128)(2,1)S(1)}, bf16[512,2048]{1,0:T(8,128)(2,1)}, u32[]{:S(2)}, u32[]{:S(2)}) %collective-permute-start.2) | collective-permute-done | bytes 2097184 | tf_op jit(solution)/shard_map/ppermute | solution.py:29
  242.5 2.6 collective-permute-start.3
  246.1 2.2 collective-permute-start.6
  248.3 86.0 %collective-permute-done.3 = bf16[512,2048]{1,0:T(8,128)(2,1)} collective-permute-done((bf16[512,2048]{1,0:T(8,128)(2,1)}, bf16[512,2048]{1,0:T(8,128)(2,1)}, u32[]{:S(2)}, u32[]{:S(2)}) %collective-permute-start.3) | collective-permute-done | bytes 2097184 | tf_op jit(solution)/shard_map/ppermute | solution.py:29
  334.3 1.8 bitcast_dynamic-update-slice_fusion.7
  336.1 1.8 bitcast_dynamic-update-slice_fusion.6
  337.9 1.8 bitcast_dynamic-update-slice_fusion.5
  339.8 1.8 bitcast_dynamic-update-slice_fusion.4
  341.8 1.8 bitcast_dynamic-update-slice_fusion.2
  343.6 1.8 bitcast_dynamic-update-slice_fusion.1
  345.6 6.5 %fusion.25 = (bf16[8,512,1024]{2,1,0:T(8,128)(2,1)}, bf16[8,512,1024]{2,1,0:T(8,128)(2,1)}) fusion(bf16[8,512,2048]{2,1,0:T(8,128)(2,1)S(1)} %bitcast_dynamic-update-slice_fusion), kind=kLoop, calls=%fused_computation.67 | loop fusion | bytes 33554432 | tf_op jit(solution)/shard_map/gather | solution.py:39
  352.1 8.1 %gather_fusion = bf16[8,512,1024]{2,1,0:T(8,128)(2,1)} fusion(bf16[8,512,1024]{2,1,0:T(8,128)(2,1)} %get-tuple-element.5, s32[1024]{0:T(1024)S(1)} %pad_clamp_fusion), kind=kCustom, calls=%fused_computation | custom fusion | bytes 16777248 | tf_op jit(solution)/shard_map/gather | solution.py:39
  360.1 8.1 %gather_fusion.1 = bf16[8,512,1024]{2,1,0:T(8,128)(2,1)} fusion(bf16[8,512,1024]{2,1,0:T(8,128)(2,1)} %get-tuple-element.6, s32[1024]{0:T(1024)S(1)} %pad_clamp_fusion), kind=kCustom, calls=%fused_computation.1 | custom fusion | bytes 16777248 | tf_op jit(solution)/shard_map/gather | solution.py:39
  368.2 7.8 %pad_maximum_fusion = bf16[8,512,2048]{2,1,0:T(8,128)(2,1)S(1)} fusion(bf16[8,512,1024]{2,1,0:T(8,128)(2,1)} %gather_fusion.1, bf16[8,512,1024]{2,1,0:T(8,128)(2,1)} %gather_fusion), kind=kLoop, calls=%fused_computation.2 | loop fusion | flops 33554432 | bytes 33554432
  376.1 5.7 %copy-done.1 = bf16[8,512,2048]{2,1,0:T(8,128)(2,1)} copy-done((bf16[8,512,2048]{2,1,0:T(8,128)(2,1)}, bf16[8,512,2048]{2,1,0:T(8,128)(2,1)S(1)}, u32[]{:S(2)}) %copy-start.1) | copy-done | bytes 16777240
  381.8 2.5 fusion
  384.3 4.4 collective-permute-start.7
  388.8 1.4 collective-permute-done.7
  392.0 9.5 %convolution_convert_fusion.1 = bf16[128,4096]{1,0:T(8,128)(2,1)} fusion(bf16[2048,4096]{1,0:T(8,128)(2,1)} %param.13, bf16[128,2048]{1,0:T(8,128)(2,1)S(1)} %copy-done.8, f32[128,2048]{1,0:T(8,128)S(1)} %fusion.10), kind=kOutput, calls=%fused_computation.4 | convolution fusion | flops 2150891520 | bytes 19398656 | tf_op jit(solution)/shard_map/dot_general | solution.py:80
  401.8 34.6 %all-reduce.8.cloned.1.call-done = bf16[128,4096]{1,0:T(8,128)(2,1)} async-done(((bf16[128,4096]{1,0:T(8,128)(2,1)}), bf16[128,4096]{1,0:T(8,128)(2,1)}) %all-reduce.8.cloned.1.call-update) | async-done | bytes 1048592 | tf_op jit(solution)/shard_map/psum | solution.py:87
  436.4 13.7 %multiply_multiply_fusion.2 = (f32[128,2048]{1,0:T(8,128)S(1)}, f32[128,2048]{1,0:T(8,128)S(1)}, bf16[128,2048]{1,0:T(8,128)(2,1)}) fusion(f32[128]{0:T(128)S(1)} %get-tuple-element.15, f32[2048]{0:T(1024)S(1)} %bitcast.39, f32[128,2048]{1,0:T(8,128)} %copy-done.6, bf16[128,2048]{1,0:T(8,128)(2,1)} %param.11, bf16[2048,4096]{1,0:T(8,128)(2,1)} %param.13, ...), kind=kOutput, calls=%fused_computation.41 | convolution fusion | flops 2156396544 | bytes 23077888 | tf_op jit(solution)/shard_map/dot_general | solution.py:90
  453.6 2.3 slice.73
  456.9 13.1 %convolution_convert_fusion = bf16[128,4096]{1,0:T(8,128)(2,1)} fusion(bf16[4096,2048]{1,0:T(8,128)(2,1)} %bitcast.31, f32[3,2048]{1,0:T(4,128)S(1)} %collective-permute-done.8, f32[125,2048]{1,0:T(8,128)} %slice.75, f32[126,2048]{1,0:T(8,128)S(1)} %slice.74, f32[127,2048]{1,0:T(8,128)} %slice.73, f32[128,2048]{1,0:T(8,128)S(1)} %get-tuple-element.4, ...), kind=kOutput, calls=%fused_computation.3 | convolution fusion | flops 2149580800 | bytes 22003712 | tf_op jit(solution)/shard_map/dot_general | solution.py:116
  470.0 1.7 dynamic-slice_convert_fusion
  471.7 23.9 %reduce-scatter.2.cloned.1.call-done = bf16[128,1024]{1,0:T(8,128)(2,1)} async-done(((bf16[128,4096]{1,0:T(8,128)(2,1)}), bf16[128,1024]{1,0:T(8,128)(2,1)}) %reduce-scatter.2.cloned.1.call-update) | async-done | bytes 262160 | tf_op jit(solution)/shard_map/reduce_scatter | solution.py:119
  (46 shorter events, 9.3 us)
Async XLA Ops:
  7.2 374.6 %copy-start = (bf16[128,4096]{1,0:T(8,128)(2,1)S(1)}, bf16[128,4096]{1,0:T(8,128)(2,1)}, u32[]{:S(2)}) copy-start(bf16[128,4096]{1,0:T(8,128)(2,1)} %param.9) | copy-start | bytes 3145732
  7.2 334.4 %copy-start.2 = (bf16[512,2048]{1,0:T(8,128)(2,1)S(1)}, bf16[512,2048]{1,0:T(8,128)(2,1)}, u32[]{:S(2)}) copy-start(bf16[512,2048]{1,0:T(8,128)(2,1)} %param.10) | copy-start | bytes 6291460
  7.2 429.2 %all-reduce.8.cloned.1.call-start = ((), (), s32[]{:S(2)}) async-start(), calls=%async_computation.1 | async-start | bytes 2097152 | tf_op jit(solution)/shard_map/psum | solution.py:87
  7.2 51.9 %collective-permute-start = (bf16[512,2048]{1,0:T(8,128)(2,1)}, bf16[512,2048]{1,0:T(8,128)(2,1)S(1)}, u32[]{:S(2)}, u32[]{:S(2)}) collective-permute-start(bf16[512,2048]{1,0:T(8,128)(2,1)} %param.10), channel_id=1, source_target_pairs={{0,4},{4,8},{8,12},{12,16},{16,20},{20,24},{24,28},{28,0},{1,5},{5... | collective-permute-start | bytes 6291464 | tf_op jit(solution)/shard_map/ppermute | solution.py:29
  59.1 1.3 copy-start.3
  60.5 89.6 %collective-permute-start.1 = (bf16[512,2048]{1,0:T(8,128)(2,1)S(1)}, bf16[512,2048]{1,0:T(8,128)(2,1)S(1)}, u32[]{:S(2)}, u32[]{:S(2)}) collective-permute-start(bf16[512,2048]{1,0:T(8,128)(2,1)S(1)} %collective-permute-done), channel_id=1, source_target_pairs={{0,4},{4,8},{8,12},{12,16},{16,20},{20,24},{24,28},{28,0},{1,5},{5... | collective-permute-start | bytes 6291464 | tf_op jit(solution)/shard_map/ppermute | solution.py:29
  60.5 93.4 %collective-permute-start.4 = (bf16[512,2048]{1,0:T(8,128)(2,1)}, bf16[512,2048]{1,0:T(8,128)(2,1)}, u32[]{:S(2)}, u32[]{:S(2)}) collective-permute-start(bf16[512,2048]{1,0:T(8,128)(2,1)} %param.10), channel_id=1, source_target_pairs={{4,0},{8,4},{12,8},{16,12},{20,16},{24,20},{28,24},{0,28},{5,1},{9... | collective-permute-start | bytes 6291464 | tf_op jit(solution)/shard_map/ppermute | solution.py:35
  150.0 1.4 copy-start.4
  151.4 91.1 %collective-permute-start.2 = (bf16[512,2048]{1,0:T(8,128)(2,1)S(1)}, bf16[512,2048]{1,0:T(8,128)(2,1)}, u32[]{:S(2)}, u32[]{:S(2)}) collective-permute-start(bf16[512,2048]{1,0:T(8,128)(2,1)S(1)} %collective-permute-done.1), channel_id=1, source_target_pairs={{0,4},{4,8},{8,12},{12,16},{16,20},{20,24},{24,28},{28,0},{1,5},{5... | collective-permute-start | bytes 6291464 | tf_op jit(solution)/shard_map/ppermute | solution.py:29
  153.9 92.2 %collective-permute-start.5 = (bf16[512,2048]{1,0:T(8,128)(2,1)}, bf16[512,2048]{1,0:T(8,128)(2,1)}, u32[]{:S(2)}, u32[]{:S(2)}) collective-permute-start(bf16[512,2048]{1,0:T(8,128)(2,1)} %collective-permute-done.4), channel_id=1, source_target_pairs={{4,0},{8,4},{12,8},{16,12},{20,16},{24,20},{28,24},{0,28},{5,1},{9... | collective-permute-start | bytes 6291464 | tf_op jit(solution)/shard_map/ppermute | solution.py:35
  242.5 91.7 %collective-permute-start.3 = (bf16[512,2048]{1,0:T(8,128)(2,1)}, bf16[512,2048]{1,0:T(8,128)(2,1)}, u32[]{:S(2)}, u32[]{:S(2)}) collective-permute-start(bf16[512,2048]{1,0:T(8,128)(2,1)} %collective-permute-done.2), channel_id=1, source_target_pairs={{0,4},{4,8},{8,12},{12,16},{16,20},{20,24},{24,28},{28,0},{1,5},{5... | collective-permute-start | bytes 6291464 | tf_op jit(solution)/shard_map/ppermute | solution.py:29
  246.1 99.4 %collective-permute-start.6 = (bf16[512,2048]{1,0:T(8,128)(2,1)}, bf16[512,2048]{1,0:T(8,128)(2,1)S(1)}, u32[]{:S(2)}, u32[]{:S(2)}) collective-permute-start(bf16[512,2048]{1,0:T(8,128)(2,1)} %collective-permute-done.5), channel_id=1, source_target_pairs={{4,0},{8,4},{12,8},{16,12},{20,16},{24,20},{28,24},{0,28},{5,1},{9... | collective-permute-start | bytes 6291464 | tf_op jit(solution)/shard_map/ppermute | solution.py:35
  376.0 5.7 %copy-start.1 = (bf16[8,512,2048]{2,1,0:T(8,128)(2,1)}, bf16[8,512,2048]{2,1,0:T(8,128)(2,1)S(1)}, u32[]{:S(2)}) copy-start(bf16[8,512,2048]{2,1,0:T(8,128)(2,1)S(1)} %pad_maximum_fusion) | copy-start | bytes 50331652
  376.1 12.7 %copy-start.7 = (s32[128]{0:T(128)S(1)}, s32[128]{0:T(128)}, u32[]{:S(2)}) copy-start(s32[128]{0:T(128)} %param.17) | copy-start | bytes 1540
  376.1 15.9 %copy-start.8 = (bf16[128,2048]{1,0:T(8,128)(2,1)S(1)}, bf16[128,2048]{1,0:T(8,128)(2,1)}, u32[]{:S(2)}) copy-start(bf16[128,2048]{1,0:T(8,128)(2,1)} %param.11) | copy-start | bytes 1572868
  384.3 5.8 %collective-permute-start.7 = (bf16[3,2048]{1,0:T(4,128)(2,1)S(1)}, bf16[3,2048]{1,0:T(4,128)(2,1)S(1)}, u32[]{:S(2)}, u32[]{:S(2)}) collective-permute-start(bf16[3,2048]{1,0:T(4,128)(2,1)S(1)} %slice.68), channel_id=1, source_target_pairs={{0,4},{4,8},{8,12},{12,16},{16,20},{20,24},{24,28},{1,5},{5,9},{9,... | collective-permute-start | bytes 36872 | tf_op jit(solution)/shard_map/ppermute | solution.py:49
  391.1 1.0 copy-start.6
  392.0 9.7 %copy-start.9 = (f32[32]{0:T(128)S(1)}, f32[32]{0:T(128)}, u32[]{:S(2)}) copy-start(f32[32]{0:T(128)} %param.16) | copy-start | bytes 388
  392.0 9.7 %copy-start.10 = (s32[128]{0:T(128)S(1)}, s32[128]{0:T(128)}, u32[]{:S(2)}) copy-start(s32[128]{0:T(128)} %param.15) | copy-start | bytes 1540
  401.5 94.0 %reduce-scatter.2.cloned.1.call-start = ((), (), s32[]{:S(2)}) async-start(), calls=%async_computation.2 | async-start | bytes 1310720 | tf_op jit(solution)/shard_map/reduce_scatter | solution.py:119
  450.1 1.0 copy-start.5
  451.1 5.8 %collective-permute-start.8 = (f32[3,2048]{1,0:T(4,128)S(1)}, f32[3,2048]{1,0:T(4,128)S(1)}, u32[]{:S(2)}, u32[]{:S(2)}) collective-permute-start(f32[3,2048]{1,0:T(4,128)S(1)} %slice_add_fusion), channel_id=1, source_target_pairs={{4,0},{8,4},{12,8},{16,12},{20,16},{24,20},{28,24},{5,1},{9,5},{13... | collective-permute-start | bytes 73736 | tf_op jit(solution)/shard_map/ppermute | solution.py:49
Sparse Core Ops, SparseCore 0:
  401.6 34.7 all-reduce.7
  470.1 25.3 reduce-scatter.1
